TPU v7x, 256 devices: a whole 4x4x8 slice. The times are simulated.
256 devices in a mesh: chan: 8 (over z_hi, x), tm: 16 (over z_lo, y), dp: 2 (over core).
Axes of the slice: x: 4, y: 4, z: 8 (z_hi: 2, z_lo: 4; z = z_hi * 4 + z_lo), core: 2. Of those that a mesh axis runs over, the one named last changes fastest.
Arguments:
- contexts: bfloat16 [512, 4, 16384], P('tm', 'dp', 'chan'), may hold values from -6 to 6
- cotangent: bfloat16 [512, 4, 16384], P('tm', 'dp', 'chan'), may hold values from -6 to 6
- w_in: bfloat16 [16384, 8192], P('chan', 'tm'), may hold values from -0.046875 to 0.046875
- w_out: bfloat16 [8192, 16384], P('tm', 'chan'), may hold values from -0.0625 to 0.0625
- time_weight: bfloat16 [512, 512], replicated, may hold values from -0.25 to 0.25
Outputs:
- grad_contexts: bfloat16 [512, 4, 16384], P('tm', 'dp', 'chan')
- grad_w_in: float32 [16384, 8192], P('chan', ('tm', 'dp'))
- grad_w_out: float32 [8192, 16384], P(('tm', 'dp'), 'chan')
- grad_time: float32 [512, 512], replicated
All inputs are finite; a program needn't handle non-finite values.
Results may differ from a plain program's by a relative error of at most 0.0057.
Values may be sent and summed in bfloat16 or wider, within the bound.
No kernel may reach another device: no remote copies, remote signals or barrier semaphores. Data moves between devices by JAX's collectives and lax.ppermute only.
A program may use at most 192 MiB of HBM per device.

v0:
```python
import math
import jax
import jax.numpy as jnp
from jax import lax
from jax.sharding import PartitionSpec as P

tanh_scale = math.sqrt(2.0 / math.pi)
cubic_term = 0.044715


def gelu_pair(value):
    inner = jnp.tanh(tanh_scale * (value + cubic_term * value * value * value))
    result = 0.5 * value * (1.0 + inner)
    slope = 0.5 * (1.0 + inner) + 0.5 * value * (1.0 - inner * inner) * tanh_scale * (
        1.0 + 3.0 * cubic_term * value * value
    )
    return (result, slope)


def hidden_finish(hidden_pre, hidden_grad):
    act_hidden, slope_hidden = gelu_pair(hidden_pre)
    return (act_hidden.astype(jnp.bfloat16), (hidden_grad * slope_hidden).astype(jnp.bfloat16))


def on_device(contexts, cotangent, w_in, w_out, time_weight):
    local_len, batch_dev, width_dev = contexts.shape
    whole_x, whole_dy = (
        lax.all_gather(contexts, "tm", axis=0, tiled=True),
        lax.all_gather(cotangent, "tm", axis=0, tiled=True),
    )
    length = whole_x.shape[0]
    flat_x = whole_x.reshape(length, batch_dev * width_dev)
    pre_time = jnp.dot(time_weight, flat_x, preferred_element_type=jnp.float32)
    act_time, slope_time = gelu_pair(pre_time)
    mixed = (
        (flat_x.astype(jnp.float32) + act_time)
        .astype(jnp.bfloat16)
        .reshape(length * batch_dev, width_dev)
    )
    grad_rows = whole_dy.reshape(length * batch_dev, width_dev)
    hidden_part = jnp.dot(mixed, w_in, preferred_element_type=jnp.float32)
    hgrad_part = jnp.einsum("rc,hc->rh", grad_rows, w_out, preferred_element_type=jnp.float32)
    hidden_pre, hidden_grad = lax.psum((hidden_part, hgrad_part), "chan")
    activation, pre_grad = hidden_finish(hidden_pre, hidden_grad)
    win_part = jnp.einsum("rc,rh->ch", mixed, pre_grad, preferred_element_type=jnp.float32)
    wout_part = jnp.einsum("rh,rc->hc", activation, grad_rows, preferred_element_type=jnp.float32)
    grad_w_in, grad_w_out = (
        lax.psum_scatter(win_part, "dp", scatter_dimension=1, tiled=True),
        lax.psum_scatter(wout_part, "dp", scatter_dimension=0, tiled=True),
    )
    position = lax.axis_index("tm")
    my_rows = local_len * batch_dev
    feature_sum = lax.psum_scatter(
        jnp.einsum("rh,ch->rc", pre_grad, w_in, preferred_element_type=jnp.float32),
        "tm",
        scatter_dimension=0,
        tiled=True,
    )
    own_dy = cotangent.reshape(my_rows, width_dev)
    mixed_grad = (own_dy.astype(jnp.float32) + feature_sum).reshape(
        local_len, batch_dev * width_dev
    )
    own_slope = lax.dynamic_slice_in_dim(slope_time, position * local_len, local_len, 0)
    own_gate = (mixed_grad * own_slope).astype(jnp.bfloat16)
    all_gate = lax.all_gather(own_gate, "tm", axis=0, tiled=True)
    own_columns = lax.dynamic_slice_in_dim(time_weight, position * local_len, local_len, 1)
    back = jnp.einsum("tl,tk->lk", own_columns, all_gate, preferred_element_type=jnp.float32)
    grad_contexts = (
        (mixed_grad + back).reshape(local_len, batch_dev, width_dev).astype(jnp.bfloat16)
    )
    time_part = jnp.einsum("tk,lk->tl", own_gate, flat_x, preferred_element_type=jnp.float32)
    time_rows = lax.psum(time_part, ("chan", "dp"))
    grad_time = lax.all_gather(time_rows, "tm", axis=0, tiled=True)
    return (grad_contexts, grad_w_in, grad_w_out, grad_time)


def solution(mesh):
    return jax.shard_map(
        on_device,
        mesh=mesh,
        in_specs=(
            P("tm", "dp", "chan"),
            P("tm", "dp", "chan"),
            P("chan", "tm"),
            P("tm", "chan"),
            P(),
        ),
        out_specs=(P("tm", "dp", "chan"), P("chan", ("tm", "dp")), P(("tm", "dp"), "chan"), P()),
        check_vma=False,
    )
```

profile of v0, /device:TPU:1, one launch (start us, length us, event | category | flops | bytes accessed | tf_op | source)
XLA Modules:
  0.0 907.4 jit_solution(18198101720754820874)
XLA Ops:
  8.7 83.0 %all-gather.7.cloned.1.call-done = bf16[512,2,2048]{2,1,0:T(2,128)(2,1)} async-done(((bf16[32,2,2048]{2,1,0:T(2,128)(2,1)}), bf16[512,2,2048]{2,1,0:T(2,128)(2,1)}) %all-gather.7.cloned.1.call-update) | async-done | bytes 4194320 | tf_op jit(solution)/shard_map/all_gather | solution.py:28
  91.7 4.6 copy.9
  96.4 14.4 %fusion.1 = (f32[512,4096]{1,0:T(8,128)}, f32[512,4096]{1,0:T(8,128)}, bf16[512,4096]{1,0:T(8,128)(2,1)}, f32[512,4096]{1,0:T(8,128)}, f32[512,4096]{1,0:T(8,128)}) fusion(bf16[512,4096]{1,0:T(8,128)(2,1)S(1)} %bitcast.16, bf16[512,512]{1,0:T(8,128)(2,1)S(1)} %copy-done.9), kind=kOutput, calls=%fused_computation.2 | convolution fusion | flops 2170552320 | bytes 42467328 | tf_op jit(solution)/shard_map/dot_general | solution.py:33
  110.7 7.1 reshape.27
  117.9 61.4 %all-gather.5.cloned.1.call-done = bf16[512,2,2048]{2,1,0:T(2,128)(2,1)} async-done(((bf16[32,2,2048]{2,1,0:T(2,128)(2,1)}), bf16[512,2,2048]{2,1,0:T(2,128)(2,1)}) %all-gather.5.cloned.1.call-update) | async-done | bytes 4194320 | tf_op jit(solution)/shard_map/all_gather | solution.py:29
  179.3 7.2 reshape.25
  186.4 6.7 fusion.28
  193.1 3.7 fusion.29
  197.0 198.9 %all-reduce.6.cloned.1.call-done = (f32[1024,512]{1,0:T(8,128)}, f32[1024,512]{1,0:T(8,128)}) async-done(((f32[1024,512]{1,0:T(8,128)}, f32[1024,512]{1,0:T(8,128)}), (f32[1024,512]{1,0:T(8,128)}, f32[1024,512]{1,0:T(8,128)})) %all-reduce.6.cloned.1.call-update) | async-done | bytes 4194320 | tf_op jit(solution)/shard_map/psum | solution.py:43
  395.9 3.5 fusion.9
  400.4 5.6 fusion.30
  407.1 101.0 %reduce-scatter.4.cloned.1.call-done = f32[64,2048]{1,0:T(8,128)} async-done(((f32[1024,2048]{1,0:T(8,128)}), f32[64,2048]{1,0:T(8,128)}) %reduce-scatter.4.cloned.1.call-update) | async-done | bytes 524304 | tf_op jit(solution)/shard_map/reduce_scatter | solution.py:53
  509.3 1.7 fusion.19
  511.1 4.3 fusion.32
  515.4 170.7 %all-reduce.4.cloned.1.call-done = f32[32,512]{1,0:T(8,128)} async-done(((f32[32,512]{1,0:T(8,128)}), f32[32,512]{1,0:T(8,128)}) %all-reduce.4.cloned.1.call-update) | async-done | bytes 65552 | tf_op jit(solution)/shard_map/psum | solution.py:72
  686.9 6.5 fusion.31
  693.5 1.5 copy-done.5
  695.0 6.7 fusion.10
  701.8 56.8 %all-gather.11.cloned.1.call-done = f32[512,512]{1,0:T(8,128)} async-done(((f32[32,512]{1,0:T(8,128)}), f32[512,512]{1,0:T(8,128)}) %all-gather.11.cloned.1.call-update) | async-done | bytes 1048592 | tf_op jit(solution)/shard_map/all_gather | solution.py:73
  758.6 89.3 %all-gather.9.cloned.1.call-done = bf16[512,4096]{1,0:T(8,128)(2,1)} async-done(((bf16[32,4096]{1,0:T(8,128)(2,1)}), bf16[512,4096]{1,0:T(8,128)(2,1)}) %all-gather.9.cloned.1.call-update) | async-done | bytes 4194320 | tf_op jit(solution)/shard_map/all_gather | solution.py:65
  848.0 3.3 fusion.2
  852.1 24.6 %reduce-scatter.6.cloned.1.call-done = f32[2048,256]{1,0:T(8,128)} async-done(((f32[2048,512]{1,0:T(8,128)}), f32[2048,256]{1,0:T(8,128)}) %reduce-scatter.6.cloned.1.call-update) | async-done | bytes 2097168 | tf_op jit(solution)/shard_map/reduce_scatter | solution.py:48
  876.7 21.9 %reduce-scatter.8.cloned.1.call-done = f32[256,2048]{1,0:T(8,128)} async-done(((f32[512,2048]{1,0:T(8,128)}), f32[256,2048]{1,0:T(8,128)}) %reduce-scatter.8.cloned.1.call-update) | async-done | bytes 2097168 | tf_op jit(solution)/shard_map/reduce_scatter | solution.py:49
  898.6 2.3 copy.14
  (41 shorter events, 6.8 us)
Async XLA Ops:
  7.2 186.0 %copy-start = (bf16[2048,512]{1,0:T(8,128)(2,1)S(1)}, bf16[2048,512]{1,0:T(8,128)(2,1)}, u32[]{:S(2)}) copy-start(bf16[2048,512]{1,0:T(8,128)(2,1)} %param.7) | copy-start | bytes 6291460
  7.2 84.5 %all-gather.7.cloned.1.call-start = ((), (), s32[]{:S(2)}) async-start(), calls=%async_computation.4 | async-start | bytes 4456448 | tf_op jit(solution)/shard_map/all_gather | solution.py:28
  7.9 171.3 %all-gather.5.cloned.1.call-start = ((), (), s32[]{:S(2)}) async-start(), calls=%async_computation.3 | async-start | bytes 4456448 | tf_op jit(solution)/shard_map/all_gather | solution.py:29
  8.7 387.2 %all-reduce.6.cloned.1.call-start = ((), (), s32[]{:S(2)}) async-start(), calls=%async_computation.11 | async-start | bytes 8388608 | tf_op jit(solution)/shard_map/psum | solution.py:43
  91.7 4.7 copy-start.9
  96.4 14.4 %copy-start.2 = (bf16[64,8,2,2048]{3,1,2,0:T(8,128)(2,1)}, bf16[64,8,2,2048]{3,1,2,0:T(8,128)(2,1)S(1)}, u32[]{:S(2)}) copy-start(bf16[64,8,2,2048]{3,1,2,0:T(8,128)(2,1)S(1)} %copy.9) | copy-start | bytes 12582916
  186.4 6.7 copy-start.3
  196.8 311.2 %reduce-scatter.4.cloned.1.call-start = ((), (), s32[]{:S(2)}) async-start(), calls=%async_computation.5 | async-start | bytes 8912896 | tf_op jit(solution)/shard_map/reduce_scatter | solution.py:53
  399.5 1.0 copy-start.6
  406.0 0.9 copy-start.8
  406.1 280.1 %all-reduce.4.cloned.1.call-start = ((), (), s32[]{:S(2)}) async-start(), calls=%async_computation.9 | async-start | bytes 131072 | tf_op jit(solution)/shard_map/psum | solution.py:72
  511.0 4.3 copy-start.4
  511.1 175.9 %copy-start.7 = (bf16[1024,512]{1,0:T(8,128)(2,1)S(1)}, bf16[1024,512]{1,0:T(8,128)(2,1)}, u32[]{:S(2)}) copy-start(bf16[1024,512]{1,0:T(8,128)(2,1)} %copy-done.6) | copy-start | bytes 3145732
  515.4 243.2 %all-gather.11.cloned.1.call-start = ((), (), s32[]{:S(2)}) async-start(), calls=%async_computation.10 | async-start | bytes 1114112 | tf_op jit(solution)/shard_map/all_gather | solution.py:73
  686.1 161.8 %all-gather.9.cloned.1.call-start = ((), (), s32[]{:S(2)}) async-start(), calls=%async_computation.6 | async-start | bytes 4456448 | tf_op jit(solution)/shard_map/all_gather | solution.py:65
  686.9 189.9 %reduce-scatter.6.cloned.1.call-start = ((), (), s32[]{:S(2)}) async-start(), calls=%async_computation.7 | async-start | bytes 6291456 | tf_op jit(solution)/shard_map/reduce_scatter | solution.py:48
  693.5 1.6 copy-start.5
  693.5 205.2 %reduce-scatter.8.cloned.1.call-start = ((), (), s32[]{:S(2)}) async-start(), calls=%async_computation.8 | async-start | bytes 6291456 | tf_op jit(solution)/shard_map/reduce_scatter | solution.py:49
  848.0 52.9 %copy-start.1 = (bf16[2048,512]{1,0:T(8,128)(2,1)S(1)}, bf16[2048,512]{1,0:T(8,128)(2,1)}, u32[]{:S(2)}) copy-start(bf16[2048,512]{1,0:T(8,128)(2,1)} %param.7) | copy-start | bytes 6291460
Sparse Core Ops, SparseCore 0:
  9.8 81.8 all-gather.6
  93.5 85.7 all-gather.4
  196.9 198.9 all-reduce.5
  406.2 101.8 reduce-scatter.3
  515.5 170.5 all-reduce.3
  687.8 70.8 all-gather.10
  761.0 86.9 all-gather.8
  851.1 25.6 reduce-scatter.5
  879.9 18.7 reduce-scatter.7
where the time goes:
time: 908 us; the launch traced here: 907 us
  waiting for transfers between devices  810 us (89%)
  matrix products  51.1 us (6%)
  local copies, waits for them, and re-layouts  25.7 us (3%)
  between operations  13.9 us (2%)
    psum x1, waiting for transfers between devices, on_device(): hidden_pre, hidden_grad = lax.psum((hidden_part, hgrad_part), 'chan')  199 us
    psum x1, waiting for transfers between devices, on_device(): time_rows = lax.psum(time_part, ('chan', 'dp'))  171 us
    reduce_scatter x1, waiting for transfers between devices, on_device(): lax.psum_scatter(jnp.einsum('rh,ch->rc', pre_grad, w_in, preferred_elemen...  101 us
    all_gather x1, waiting for transfers between devices, on_device(): all_gate = lax.all_gather(own_gate, 'tm', axis=0, tiled=True)  89.3 us
    all_gather x1, waiting for transfers between devices, on_device(): lax.all_gather(contexts, 'tm', axis=0, tiled=True)  83 us
    all_gather x1, waiting for transfers between devices, on_device(): lax.all_gather(cotangent, 'tm', axis=0, tiled=True)  61.4 us
    all_gather x1, waiting for transfers between devices, on_device(): grad_time = lax.all_gather(time_rows, 'tm', axis=0, tiled=True)  56.8 us
    reduce_scatter x1, waiting for transfers between devices, on_device(): lax.psum_scatter(win_part, 'dp', scatter_dimension=1, tiled=True)  24.6 us
  transfers between devices with their start and end apart: 9, of which 9 were waited for; matrix products, arithmetic and copies ran while one was open for 5% of the time, Pallas kernels for 0%

commit v1 on v0

--- a/solution.py
+++ b/solution.py
@@ -69,7 +69,7 @@
         (mixed_grad + back).reshape(local_len, batch_dev, width_dev).astype(jnp.bfloat16)
     )
     time_part = jnp.einsum("tk,lk->tl", own_gate, flat_x, preferred_element_type=jnp.float32)
-    time_rows = lax.psum(time_part, ("chan", "dp"))
+    time_rows = jnp.sum(lax.all_gather(time_part, ("chan", "dp")), axis=0)
     grad_time = lax.all_gather(time_rows, "tm", axis=0, tiled=True)
     return (grad_contexts, grad_w_in, grad_w_out, grad_time)
 

time: 908 us -> 793 us (0.87)
  waiting for transfers between devices: 810 us -> 693 us
    psum x1 -> x0, waiting for transfers between devices: 171 us -> none  [on_device(): time_rows = lax.psum(time_part, ('chan', 'dp'))]
    all_gather x0 -> x1, waiting for transfers between devices: none -> 60.7 us  [on_device(): time_rows = jnp.sum(lax.all_gather(time_part, ('chan', 'dp')), axis=0)]
  transfers between devices with their start and end apart: 9 -> 9, of which waited for: 9 -> 9; matrix products, arithmetic and copies ran while one was open for 5% -> 6% of each run, Pallas kernels for 0% -> 0%
where the time goes in v1:
time: 793 us
  waiting for transfers between devices  693 us (87%)
  matrix products  51.1 us (6%)
  local copies, waits for them, and re-layouts  25.7 us (3%)
  between operations  13.9 us (2%)
  other arithmetic  8.28 us (1%)
    psum x1, waiting for transfers between devices, on_device(): hidden_pre, hidden_grad = lax.psum((hidden_part, hgrad_part), 'chan')  199 us
    reduce_scatter x1, waiting for transfers between devices, on_device(): lax.psum_scatter(jnp.einsum('rh,ch->rc', pre_grad, w_in, preferred_elemen...  101 us
    all_gather x1, waiting for transfers between devices, on_device(): all_gate = lax.all_gather(own_gate, 'tm', axis=0, tiled=True)  89.3 us
    all_gather x1, waiting for transfers between devices, on_device(): lax.all_gather(contexts, 'tm', axis=0, tiled=True)  83 us
    all_gather x1, waiting for transfers between devices, on_device(): lax.all_gather(cotangent, 'tm', axis=0, tiled=True)  61.4 us
    all_gather x1, waiting for transfers between devices, on_device(): time_rows = jnp.sum(lax.all_gather(time_part, ('chan', 'dp')), axis=0)  60.7 us
    all_gather x1, waiting for transfers between devices, on_device(): grad_time = lax.all_gather(time_rows, 'tm', axis=0, tiled=True)  50 us
    reduce_scatter x1, waiting for transfers between devices, on_device(): lax.psum_scatter(win_part, 'dp', scatter_dimension=1, tiled=True)  24.6 us
  transfers between devices with their start and end apart: 9, of which 9 were waited for; matrix products, arithmetic and copies ran while one was open for 6% of the time, Pallas kernels for 0%

profile of v1, /device:TPU:1, one launch (start us, length us, event | category | flops | bytes accessed | tf_op | source)
XLA Modules:
  0.0 792.6 jit_solution(6420958457680240411)
XLA Ops:
  8.7 83.0 %all-gather.9.cloned.1.call-done = bf16[512,2,2048]{2,1,0:T(2,128)(2,1)} async-done(((bf16[32,2,2048]{2,1,0:T(2,128)(2,1)}), bf16[512,2,2048]{2,1,0:T(2,128)(2,1)}) %all-gather.9.cloned.1.call-update) | async-done | bytes 4194320 | tf_op jit(solution)/shard_map/all_gather | solution.py:28
  91.7 4.6 copy.9
  96.4 14.4 %fusion.1 = (f32[512,4096]{1,0:T(8,128)}, f32[512,4096]{1,0:T(8,128)}, bf16[512,4096]{1,0:T(8,128)(2,1)}, f32[512,4096]{1,0:T(8,128)}, f32[512,4096]{1,0:T(8,128)}) fusion(bf16[512,4096]{1,0:T(8,128)(2,1)S(1)} %bitcast.17, bf16[512,512]{1,0:T(8,128)(2,1)S(1)} %copy-done.9), kind=kOutput, calls=%fused_computation.2 | convolution fusion | flops 2170552320 | bytes 42467328 | tf_op jit(solution)/shard_map/dot_general | solution.py:33
  110.7 7.1 reshape.27
  117.9 61.4 %all-gather.7.cloned.1.call-done = bf16[512,2,2048]{2,1,0:T(2,128)(2,1)} async-done(((bf16[32,2,2048]{2,1,0:T(2,128)(2,1)}), bf16[512,2,2048]{2,1,0:T(2,128)(2,1)}) %all-gather.7.cloned.1.call-update) | async-done | bytes 4194320 | tf_op jit(solution)/shard_map/all_gather | solution.py:29
  179.3 7.2 reshape.25
  186.4 6.7 fusion.28
  193.1 3.7 fusion.29
  197.0 198.9 %all-reduce.3.cloned.1.call-done = (f32[1024,512]{1,0:T(8,128)}, f32[1024,512]{1,0:T(8,128)}) async-done(((f32[1024,512]{1,0:T(8,128)}, f32[1024,512]{1,0:T(8,128)}), (f32[1024,512]{1,0:T(8,128)}, f32[1024,512]{1,0:T(8,128)})) %all-reduce.3.cloned.1.call-update) | async-done | bytes 4194320 | tf_op jit(solution)/shard_map/psum | solution.py:43
  395.9 3.5 fusion.9
  400.4 5.6 fusion.30
  407.1 101.0 %reduce-scatter.4.cloned.1.call-done = f32[64,2048]{1,0:T(8,128)} async-done(((f32[1024,2048]{1,0:T(8,128)}), f32[64,2048]{1,0:T(8,128)}) %reduce-scatter.4.cloned.1.call-update) | async-done | bytes 524304 | tf_op jit(solution)/shard_map/reduce_scatter | solution.py:53
  509.3 1.7 fusion.19
  511.1 4.3 fusion.32
  515.4 60.7 %all-gather.15.cloned.1.call-done = f32[512,512]{1,0:T(8,128)} async-done(((f32[32,512]{1,0:T(8,128)}), f32[512,512]{1,0:T(8,128)}) %all-gather.15.cloned.1.call-update) | async-done | bytes 1048592 | tf_op jit(solution)/shard_map/all_gather | solution.py:72
  576.1 1.9 reduce_sum.9
  578.9 6.6 fusion.31
  587.1 6.7 fusion.10
  593.8 50.0 %all-gather.13.cloned.1.call-done = f32[512,512]{1,0:T(8,128)} async-done(((f32[32,512]{1,0:T(8,128)}), f32[512,512]{1,0:T(8,128)}) %all-gather.13.cloned.1.call-update) | async-done | bytes 1048592 | tf_op jit(solution)/shard_map/all_gather | solution.py:73
  643.8 89.3 %all-gather.11.cloned.1.call-done = bf16[512,4096]{1,0:T(8,128)(2,1)} async-done(((bf16[32,4096]{1,0:T(8,128)(2,1)}), bf16[512,4096]{1,0:T(8,128)(2,1)}) %all-gather.11.cloned.1.call-update) | async-done | bytes 4194320 | tf_op jit(solution)/shard_map/all_gather | solution.py:65
  733.1 3.3 fusion.2
  737.3 24.6 %reduce-scatter.6.cloned.1.call-done = f32[2048,256]{1,0:T(8,128)} async-done(((f32[2048,512]{1,0:T(8,128)}), f32[2048,256]{1,0:T(8,128)}) %reduce-scatter.6.cloned.1.call-update) | async-done | bytes 2097168 | tf_op jit(solution)/shard_map/reduce_scatter | solution.py:48
  761.9 21.9 %reduce-scatter.8.cloned.1.call-done = f32[256,2048]{1,0:T(8,128)} async-done(((f32[512,2048]{1,0:T(8,128)}), f32[256,2048]{1,0:T(8,128)}) %reduce-scatter.8.cloned.1.call-update) | async-done | bytes 2097168 | tf_op jit(solution)/shard_map/reduce_scatter | solution.py:49
  783.8 2.3 copy.13
  (42 shorter events, 8.3 us)
Async XLA Ops:
  7.2 186.0 %copy-start = (bf16[2048,512]{1,0:T(8,128)(2,1)S(1)}, bf16[2048,512]{1,0:T(8,128)(2,1)}, u32[]{:S(2)}) copy-start(bf16[2048,512]{1,0:T(8,128)(2,1)} %param.7) | copy-start | bytes 6291460
  7.2 84.5 %all-gather.9.cloned.1.call-start = ((), (), s32[]{:S(2)}) async-start(), calls=%async_computation.4 | async-start | bytes 4456448 | tf_op jit(solution)/shard_map/all_gather | solution.py:28
  7.9 171.3 %all-gather.7.cloned.1.call-start = ((), (), s32[]{:S(2)}) async-start(), calls=%async_computation.3 | async-start | bytes 4456448 | tf_op jit(solution)/shard_map/all_gather | solution.py:29
  8.7 387.2 %all-reduce.3.cloned.1.call-start = ((), (), s32[]{:S(2)}) async-start(), calls=%async_computation.11 | async-start | bytes 8388608 | tf_op jit(solution)/shard_map/psum | solution.py:43
  91.7 4.7 copy-start.9
  96.4 14.4 %copy-start.2 = (bf16[64,8,2,2048]{3,1,2,0:T(8,128)(2,1)}, bf16[64,8,2,2048]{3,1,2,0:T(8,128)(2,1)S(1)}, u32[]{:S(2)}) copy-start(bf16[64,8,2,2048]{3,1,2,0:T(8,128)(2,1)S(1)} %copy.9) | copy-start | bytes 12582916
  186.4 6.7 copy-start.3
  196.8 311.2 %reduce-scatter.4.cloned.1.call-start = ((), (), s32[]{:S(2)}) async-start(), calls=%async_computation.5 | async-start | bytes 8912896 | tf_op jit(solution)/shard_map/reduce_scatter | solution.py:53
  399.5 1.0 copy-start.6
  406.0 0.9 copy-start.8
  406.1 170.1 %all-gather.15.cloned.1.call-start = ((), (), s32[]{:S(2)}) async-start(), calls=%async_computation.10 | async-start | bytes 1114112 | tf_op jit(solution)/shard_map/all_gather | solution.py:72
  511.0 4.3 copy-start.4
  511.1 67.8 %copy-start.7 = (bf16[1024,512]{1,0:T(8,128)(2,1)S(1)}, bf16[1024,512]{1,0:T(8,128)(2,1)}, u32[]{:S(2)}) copy-start(bf16[1024,512]{1,0:T(8,128)(2,1)} %copy-done.6) | copy-start | bytes 3145732
  515.4 128.4 %all-gather.13.cloned.1.call-start = ((), (), s32[]{:S(2)}) async-start(), calls=%async_computation.9 | async-start | bytes 1114112 | tf_op jit(solution)/shard_map/all_gather | solution.py:73
  578.1 155.1 %all-gather.11.cloned.1.call-start = ((), (), s32[]{:S(2)}) async-start(), calls=%async_computation.6 | async-start | bytes 4456448 | tf_op jit(solution)/shard_map/all_gather | solution.py:65
  578.8 183.1 %reduce-scatter.6.cloned.1.call-start = ((), (), s32[]{:S(2)}) async-start(), calls=%async_computation.7 | async-start | bytes 6291456 | tf_op jit(solution)/shard_map/reduce_scatter | solution.py:48
  585.5 1.6 copy-start.5
  585.5 198.3 %reduce-scatter.8.cloned.1.call-start = ((), (), s32[]{:S(2)}) async-start(), calls=%async_computation.8 | async-start | bytes 6291456 | tf_op jit(solution)/shard_map/reduce_scatter | solution.py:49
  733.1 52.9 %copy-start.1 = (bf16[2048,512]{1,0:T(8,128)(2,1)S(1)}, bf16[2048,512]{1,0:T(8,128)(2,1)}, u32[]{:S(2)}) copy-start(bf16[2048,512]{1,0:T(8,128)(2,1)} %param.7) | copy-start | bytes 6291460
Sparse Core Ops, SparseCore 0:
  9.8 81.8 all-gather.8
  93.5 85.7 all-gather.6
  196.9 198.9 all-reduce.2
  406.2 101.8 reduce-scatter.3
  515.5 60.5 all-gather.14
  578.2 65.5 all-gather.12
  646.2 86.9 all-gather.10
  736.3 25.6 reduce-scatter.5
  765.0 18.7 reduce-scatter.7
